TPU v7x, 32 devices: a whole 2x2x4 slice. The times are simulated.
32 devices in a mesh: pipe: 4 (over x, core), tensor: 8 (over z, y).
Axes of the slice: x: 2, y: 2, z: 4, core: 2. Of those that a mesh axis runs over, the one named last changes fastest.
Arguments:
- stretch: bfloat16 [768, 7168], P(('pipe', 'tensor')), may hold values from -6 to 6
- ln_gain: float32 [7168], replicated, may hold values from 0.5 to 1.5
- ln_bias: float32 [7168], replicated, may hold values from -1.75 to 1.75
- qkv_weight: bfloat16 [7168, 12288], P(None, 'tensor'), may hold values from -0.0625 to 0.0625
- qkv_bias: float32 [12288], P('tensor'), may hold values from -1.75 to 1.75
- out_weight: bfloat16 [4096, 7168], P('tensor'), may hold values from -0.09375 to 0.09375
- out_bias: float32 [7168], replicated, may hold values from -1.75 to 1.75
- segment_ids: int32 [768], P('pipe'), may hold values from 0 to 31, never falling along the last dimension, each value on 1 to 96 neighbouring positions
- prefill_cache: bfloat16 [1, 32, 2, 128, 4096], P(None, ('pipe', 'tensor')), may hold values from -6 to 6
- block_dest: int32 [1, 32, 1], P(None, 'pipe'), may hold values from 0 to 3; in each aligned block of 8 rows (0 to 7, 8 to 15, ..., all dimensions but the last counted through in order) at most 3 rows name the same one
Outputs:
- mixed: bfloat16 [768, 7168], P(('pipe', 'tensor'))
- decode_side_cache: bfloat16 [1, 48, 2, 128, 4096], P(None, 'pipe', None, None, 'tensor')
Inputs may be any that keep to these rules, and one draw needn't show every extreme that they name: `block_dest`: among the 8 blocks of one group and one layer no decode group is named more than 3 times, and some decode group exactly 3 times. `segment_ids`: never falling along the tokens; a request spans at most 96 tokens.
All inputs are finite; a program needn't handle non-finite values.
Results may differ from a plain program's by a relative error of at most 0.013.
Values may be sent and summed in bfloat16 or wider, within the bound.
No kernel may reach another device: no remote copies, remote signals or barrier semaphores. Data moves between devices by JAX's collectives and lax.ppermute only.
A program may use at most 128 MiB of HBM per device.

v0:
```python
import jax
import jax.numpy as jnp
from jax import lax
from jax.sharding import PartitionSpec as P

HD = 128
RELAY_STEP = 0
CACHE_STEP = 2
CHAIN_PARTNER = True
CHAIN_RELAY = True


def normalize(x, gain, shift):
    mean = jnp.mean(x, axis=-1, keepdims=True)
    var = jnp.mean((x - mean) * (x - mean), axis=-1, keepdims=True)
    return ((x - mean) * lax.rsqrt(var + 1e-05) * gain + shift).astype(jnp.bfloat16)


def shifted(x, axis, k, n):
    return lax.ppermute(x, axis, [(j, (j + k) % n) for j in range(n)])


def split_heads(prefill_cache):
    tensor_count = lax.axis_size("tensor")
    layers, _, two, blk, width = prefill_cache.shape
    local_heads = width // tensor_count // HD
    split = prefill_cache.reshape(layers, two, blk, tensor_count, local_heads, HD)
    return jnp.transpose(split, (0, 1, 4, 3, 2, 5))


def send_decode(per_head_rows, block_dest):
    layers, two, local_heads, row_blocks, blk, _ = per_head_rows.shape
    pipe_count = lax.axis_size("pipe")
    capacity = 3 * row_blocks // (2 * pipe_count)
    dest = block_dest[:, :, 0]
    onehot = (dest[:, :, None] == jnp.arange(pipe_count, dtype=jnp.int32)[None, None, :]).astype(
        jnp.int32
    )
    earlier_tokens = jnp.cumsum(onehot, axis=1) - onehot
    slot = jnp.sum(earlier_tokens * onehot, axis=-1)
    position = dest * capacity + slot
    i = lax.axis_index("pipe")
    outgoing = []
    for k in range(pipe_count):
        targets = (i + k) % pipe_count * capacity + jnp.arange(capacity, dtype=jnp.int32)
        placement_index = (position[:, None, :] == targets[None, :, None]).astype(jnp.bfloat16)
        piece = jnp.einsum(
            "gud,gohdtc->guothc", placement_index, per_head_rows, preferred_element_type=jnp.float32
        ).astype(jnp.bfloat16)
        outgoing.append(piece.reshape((layers, capacity, two, blk, local_heads * HD)))
    return outgoing


def receive_decode(outgoing):
    pipe_count = lax.axis_size("pipe")
    i = lax.axis_index("pipe")
    layers, capacity = outgoing[0].shape[:2]
    arrived = jnp.zeros((layers, pipe_count * capacity) + outgoing[0].shape[2:], outgoing[0].dtype)
    previous = None
    for k in range(pipe_count):
        piece = outgoing[k]
        if k > 0:
            if previous is not None and CHAIN_RELAY:
                piece, previous = lax.optimization_barrier((piece, previous))
            piece = shifted(piece, "pipe", k, pipe_count)
            previous = piece
        arrived = lax.dynamic_update_slice_in_dim(
            arrived, piece, (i - k) % pipe_count * capacity, axis=1
        )
    return arrived


def partner(x):
    tensor_count = lax.axis_size("tensor")
    return lax.ppermute(x, "tensor", [(j, j ^ 1) for j in range(tensor_count)])


def ring(x):
    tensor_count = lax.axis_size("tensor")
    rows = tensor_count // 2
    return lax.ppermute(
        x, "tensor", [(j, (j // 2 + 1) % rows * 2 + j % 2) for j in range(tensor_count)]
    )


def gather_tokens(x, rider):
    tensor_count = lax.axis_size("tensor")
    rows = tensor_count // 2
    i = lax.axis_index("tensor")
    outer, inner = (i // 2, i % 2)
    own = [x]
    for k in range(1, rows):
        own.append(ring(own[-1]))
        if k == CACHE_STEP:
            own[-1], rider = lax.optimization_barrier((own[-1], rider))
    other = [partner(piece) for piece in own]
    steps = jnp.arange(rows)
    source = jnp.concatenate(
        [(outer - steps) % rows * 2 + inner, (outer - steps) % rows * 2 + (1 - inner)]
    )
    return (jnp.concatenate(own + other, axis=0), source, rider)


def scatter_tokens(partial, rider):
    tensor_count = lax.axis_size("tensor")
    rows = tensor_count // 2
    kept = partial[0].reshape((rows, -1) + partial[0].shape[1:])
    sent = partial[1].astype(jnp.bfloat16).reshape((rows, -1) + partial[1].shape[1:])
    mine = [None] * rows
    previous = None
    for s in [(s + 1) % rows for s in range(rows)]:
        piece = sent[s]
        if previous is not None and CHAIN_PARTNER:
            piece, previous = lax.optimization_barrier((piece, previous))
        previous = partner(piece)
        mine[s] = kept[s] + previous.astype(jnp.float32)
    carried = mine[1 % rows]
    for k in range(1, rows):
        if k == RELAY_STEP:
            carried, rider = lax.optimization_barrier((carried, rider))
        arrived = ring(carried.astype(jnp.bfloat16)).astype(jnp.float32)
        carried = arrived + mine[(k + 1) % rows]
    return (carried, rider)


def local(
    stretch,
    ln_gain,
    ln_bias,
    qkv_weight,
    qkv_bias,
    out_weight,
    out_bias,
    segment_ids,
    prefill_cache,
    block_dest,
):
    hidden = stretch.astype(jnp.float32)
    head_count = qkv_weight.shape[1] // (3 * HD)
    normed = normalize(hidden, ln_gain, ln_bias)
    split = split_heads(prefill_cache)
    gathered, source, split = gather_tokens(normed, split)
    if CACHE_STEP == 0:
        gathered, split = lax.optimization_barrier((gathered, split))
    per_head_rows = lax.all_to_all(split, "tensor", split_axis=3, concat_axis=3, tiled=True)
    outgoing = send_decode(per_head_rows, block_dest)
    qkv = (jnp.dot(gathered, qkv_weight, preferred_element_type=jnp.float32) + qkv_bias).astype(
        jnp.bfloat16
    )
    group_tokens = qkv.shape[0]
    place = (source[:, None] * normed.shape[0] + jnp.arange(normed.shape[0])[None, :]).reshape(-1)
    first_segment = segment_ids[0]
    segment_ids = segment_ids[place]
    heads = qkv.reshape(group_tokens, head_count, 3, HD)
    query = heads[:, :, 0]
    keys = heads[:, :, 1]
    value_rows = heads[:, :, 2]
    finished = per_head_rows[0]
    prefix_length = finished.shape[2] * finished.shape[3]
    cached_keys = finished[0].reshape(head_count, prefix_length, HD)
    old_values = finished[1].reshape(head_count, prefix_length, HD)
    scale = HD ** (-0.5)
    own_scores = jnp.einsum("qhd,khd->hqk", query, keys, preferred_element_type=jnp.float32) * scale
    old_scores = (
        jnp.einsum("qhd,hkd->hqk", query, cached_keys, preferred_element_type=jnp.float32) * scale
    )
    own_visible = (segment_ids[:, None] == segment_ids[None, :]) & (
        place[None, :] <= place[:, None]
    )
    old_visible = (segment_ids == first_segment)[:, None]
    own_scores = jnp.where(own_visible[None], own_scores, -jnp.inf)
    old_scores = jnp.where(old_visible[None], old_scores, -jnp.inf)
    scores = jnp.concatenate([old_scores, own_scores], axis=2)
    weights = jax.nn.softmax(scores, axis=-1).astype(jnp.bfloat16)
    context = jnp.einsum(
        "hqk,hkd->qhd",
        weights[:, :, :prefix_length],
        old_values,
        preferred_element_type=jnp.float32,
    )
    context = context + jnp.einsum(
        "hqk,khd->qhd",
        weights[:, :, prefix_length:],
        value_rows,
        preferred_element_type=jnp.float32,
    )
    context = context.astype(jnp.bfloat16).reshape(group_tokens, head_count * HD)
    decode_side_cache = receive_decode(outgoing)
    half = context.shape[0] // 2
    summed, decode_side_cache = scatter_tokens(
        [
            jnp.dot(context[:half], out_weight, preferred_element_type=jnp.float32),
            jnp.dot(context[half:], out_weight, preferred_element_type=jnp.bfloat16),
        ],
        decode_side_cache,
    )
    mixed = (hidden + summed + out_bias).astype(jnp.bfloat16)
    return (mixed, decode_side_cache)


def solution(mesh):
    return jax.shard_map(
        local,
        mesh=mesh,
        in_specs=(
            P(("pipe", "tensor"), None),
            P(),
            P(),
            P(None, "tensor"),
            P("tensor"),
            P("tensor", None),
            P(),
            P("pipe"),
            P(None, ("pipe", "tensor"), None, None, None),
            P(None, "pipe", None),
        ),
        out_specs=(P(("pipe", "tensor"), None), P(None, "pipe", None, None, "tensor")),
        check_vma=False,
    )
```

profile of v0, /device:TPU:1, one launch (start us, length us, event | category | flops | bytes accessed | tf_op | source)
XLA Modules:
  0.0 148.5 jit_solution(5265712922754977024)
XLA Ops:
  3.1 1.9 %constant_dynamic-update-slice_fusion.7 = (bf16[192,7168]{1,0:T(8,128)(2,1)}, bf16[24,7168]{1,0:T(8,128)(2,1)S(1)}) fusion(f32[7168]{0:T(1024)} %param.12, f32[7168]{0:T(1024)} %param.11, f32[24]{0:T(128)S(1)} %add_rsqrt_fusion, f32[24]{0:T(128)S(1)} %broadcast_multiply_fusion, bf16[24,7168]{1,0:T(8,128)(2,1)} %param.10), kind=kLoop, calls=%fused_computation.77 | loop fusion | flops 1032191 | bytes 1089728
  5.0 2.1 %collective-permute-start = (bf16[24,7168]{1,0:T(8,128)(2,1)S(1)}, bf16[24,7168]{1,0:T(8,128)(2,1)S(1)}, u32[]{:S(2)}, u32[]{:S(2)}) collective-permute-start(bf16[24,7168]{1,0:T(8,128)(2,1)S(1)} %get-tuple-element.17), channel_id=1, source_target_pairs={{0,2},{1,3},{2,4},{3,5},{4,6},{5,7},{6,0},{7,1},{8,10},{9,11},{10,... | collective-permute-start | bytes 1032200 | tf_op jit(solution)/shard_map/ppermute | solution.py:81
  9.8 2.0 %gather_fusion = s32[192]{0:T(256)S(1)} fusion(s32[192]{0:T(256)} %param.17, s32[1024]{0:T(1024)S(1)} %pad_clamp_fusion), kind=kCustom, calls=%fused_computation | custom fusion | bytes 2304 | tf_op jit(solution)/shard_map/gather | solution.py:153
  12.8 3.1 %copy.52 = bf16[1,1,2,128,4096]{3,4,2,1,0:T(8,128)(2,1)S(1)} copy(bf16[1,1,2,128,4096]{4,3,2,1,0:T(8,128)(2,1)} %param.18) | data formatting | bytes 4194304 | tf_op args[8]
  18.7 8.4 %collective-permute-done.1 = bf16[24,7168]{1,0:T(8,128)(2,1)S(1)} collective-permute-done((bf16[24,7168]{1,0:T(8,128)(2,1)S(1)}, bf16[24,7168]{1,0:T(8,128)(2,1)S(1)}, u32[]{:S(2)}, u32[]{:S(2)}) %collective-permute-start.1) | collective-permute-done | bytes 344096 | tf_op jit(solution)/shard_map/ppermute | solution.py:81
  28.6 2.6 %copy.53 = bf16[1,2,4,8,128,128]{5,4,2,1,0,3:T(8,128)(2,1)} copy(bf16[1,2,4,8,128,128]{4,5,2,3,1,0:T(8,128)(2,1)S(1)} %bitcast.110) | data formatting | bytes 4194304 | tf_op jit(solution)/shard_map/optimization_barrier | solution.py:95
  31.2 5.0 %all-to-all-start = ((bf16[1,2,4,8,128,128]{5,4,2,1,0,3:T(8,128)(2,1)}), bf16[1,2,4,8,128,128]{5,4,2,1,0,3:T(8,128)(2,1)S(1)}, u32[]{:S(2)}, u32[]{:S(2)}) async-start(bf16[1,2,4,8,128,128]{5,4,2,1,0,3:T(8,128)(2,1)} %copy.53), calls=%async_computation | async-start | bytes 4194304 | tf_op jit(solution)/shard_map/all_to_all | solution.py:145
  37.7 1.8 %constant_dynamic-update-slice_fusion.4 = bf16[192,7168]{1,0:T(8,128)(2,1)} fusion(bf16[192,7168]{1,0:T(8,128)(2,1)} %constant_dynamic-update-slice_fusion.5, bf16[24,7168]{1,0:T(8,128)(2,1)} %collective-permute-done.2), kind=kLoop, calls=%fused_computation.74 | loop fusion | bytes 688128
  40.2 1.7 %constant_dynamic-update-slice_fusion.2 = bf16[192,7168]{1,0:T(8,128)(2,1)} fusion(bf16[192,7168]{1,0:T(8,128)(2,1)} %constant_dynamic-update-slice_fusion.3, bf16[24,7168]{1,0:T(8,128)(2,1)} %collective-permute-done.4), kind=kLoop, calls=%fused_computation.72 | loop fusion | bytes 688128
  42.0 1.7 %constant_dynamic-update-slice_fusion.1 = bf16[192,7168]{1,0:T(8,128)(2,1)} fusion(bf16[192,7168]{1,0:T(8,128)(2,1)} %constant_dynamic-update-slice_fusion.2, bf16[24,7168]{1,0:T(8,128)(2,1)} %collective-permute-done.5), kind=kLoop, calls=%fused_computation.71 | loop fusion | bytes 688128
  43.7 18.3 %collective-permute-done.6 = bf16[24,7168]{1,0:T(8,128)(2,1)S(1)} collective-permute-done((bf16[24,7168]{1,0:T(8,128)(2,1)}, bf16[24,7168]{1,0:T(8,128)(2,1)S(1)}, u32[]{:S(2)}, u32[]{:S(2)}) %collective-permute-start.6) | collective-permute-done | bytes 344096 | tf_op jit(solution)/shard_map/ppermute | solution.py:75
  62.7 13.3 %fusion.2 = bf16[192,1536]{1,0:T(8,128)(2,1)} fusion(bf16[192,7168]{1,0:T(8,128)(2,1)} %constant_dynamic-update-slice_fusion, bf16[7168,1536]{1,0:T(8,128)(2,1)} %param.13, f32[1536]{0:T(1024)S(1)} %copy-done.7), kind=kOutput, calls=%fused_computation.7 | convolution fusion | flops 4228448256 | bytes 25368576 | tf_op jit(solution)/shard_map/dot_general | solution.py:147
  76.0 1.4 reshape.417
  79.4 2.2 %all-to-all-done = bf16[1,2,4,8,128,128]{5,4,2,1,0,3:T(8,128)(2,1)S(1)} async-done(((bf16[1,2,4,8,128,128]{5,4,2,1,0,3:T(8,128)(2,1)}), bf16[1,2,4,8,128,128]{5,4,2,1,0,3:T(8,128)(2,1)S(1)}, u32[]{:S(2)}, u32[]{:S(2)}) %all-to-all-start) | async-done | bytes 2097184 | tf_op jit(solution)/shard_map/all_to_all | solution.py:145
  89.0 3.4 %collective-permute-start.7 = (bf16[24,7168]{1,0:T(8,128)(2,1)S(1)}, bf16[24,7168]{1,0:T(8,128)(2,1)S(1)}, u32[]{:S(2)}, u32[]{:S(2)}) collective-permute-start(bf16[24,7168]{1,0:T(8,128)(2,1)S(1)} %get-tuple-element.20), channel_id=1, source_target_pairs={{0,1},{1,0},{2,3},{3,2},{4,5},{5,4},{6,7},{7,6},{8,9},{9,8},{10,11... | collective-permute-start | bytes 1032200 | tf_op jit(solution)/shard_map/ppermute | solution.py:75
  93.8 4.7 %collective-permute-done.7 = bf16[24,7168]{1,0:T(8,128)(2,1)S(1)} collective-permute-done((bf16[24,7168]{1,0:T(8,128)(2,1)S(1)}, bf16[24,7168]{1,0:T(8,128)(2,1)S(1)}, u32[]{:S(2)}, u32[]{:S(2)}) %collective-permute-start.7) | collective-permute-done | bytes 344096 | tf_op jit(solution)/shard_map/ppermute | solution.py:75
  98.5 2.0 %collective-permute-start.9 = (bf16[24,7168]{1,0:T(8,128)(2,1)}, bf16[24,7168]{1,0:T(8,128)(2,1)S(1)}, u32[]{:S(2)}, u32[]{:S(2)}) collective-permute-start(bf16[24,7168]{1,0:T(8,128)(2,1)} %get-tuple-element.11), channel_id=1, source_target_pairs={{0,1},{1,0},{2,3},{3,2},{4,5},{5,4},{6,7},{7,6},{8,9},{9,8},{10,11... | collective-permute-start | bytes 1032200 | tf_op jit(solution)/shard_map/ppermute | solution.py:75
  101.4 1.5 fusion.31
  104.1 3.3 %collective-permute-start.14 = (bf16[1,3,2,128,512]{3,4,2,1,0:T(8,128)(2,1)}, bf16[1,3,2,128,512]{3,4,2,1,0:T(8,128)(2,1)}, u32[]{:S(2)}, u32[]{:S(2)}) collective-permute-start(bf16[1,3,2,128,512]{3,4,2,1,0:T(8,128)(2,1)} %bitcast.115), channel_id=1, source_target_pairs={{0,8},{8,16},{16,24},{24,0},{1,9},{9,17},{17,25},{25,1},{2,10},{10... | collective-permute-start | bytes 2359304 | tf_op jit(solution)/shard_map/ppermute | solution.py:20
  107.9 2.5 %collective-permute-done.8 = bf16[24,7168]{1,0:T(8,128)(2,1)} collective-permute-done((bf16[24,7168]{1,0:T(8,128)(2,1)}, bf16[24,7168]{1,0:T(8,128)(2,1)}, u32[]{:S(2)}, u32[]{:S(2)}) %collective-permute-start.8) | collective-permute-done | bytes 344096 | tf_op jit(solution)/shard_map/ppermute | solution.py:81
  110.3 2.0 %fusion.63 = bf16[24,7168]{1,0:T(8,128)(2,1)} fusion(f32[96,7168]{1,0:T(8,128)} %copy-done, bf16[24,7168]{1,0:T(8,128)(2,1)S(1)} %collective-permute-done.9, bf16[24,7168]{1,0:T(8,128)(2,1)} %collective-permute-done.8), kind=kLoop, calls=%fused_computation.53 | loop fusion | flops 860160 | bytes 1720320 | tf_op jit(solution)/shard_map/convert_element_type | solution.py:121
  112.4 1.4 fusion.28
  115.2 1.4 fusion.34
  117.5 3.1 %collective-permute-done.10 = bf16[24,7168]{1,0:T(8,128)(2,1)} collective-permute-done((bf16[24,7168]{1,0:T(8,128)(2,1)}, bf16[24,7168]{1,0:T(8,128)(2,1)}, u32[]{:S(2)}, u32[]{:S(2)}) %collective-permute-start.10) | collective-permute-done | bytes 344096 | tf_op jit(solution)/shard_map/ppermute | solution.py:81
  120.6 1.4 fusion.61
  123.0 2.4 %fusion.25 = bf16[1,3,2,128,4,128]{5,1,3,4,2,0:T(4,128)(2,1)} fusion(bf16[1,2,4,8,128,128]{5,4,2,1,0,3:T(8,128)(2,1)S(1)} %all-to-all-done, s32[8]{0:T(128)S(1)} %multiply_add_fusion, s32[3]{0:T(128)S(1)} %iota_add_fusion.1), kind=kOutput, calls=%fused_computation.22 | convolution fusion | flops 6684696 | bytes 2883628 | tf_op jit(solution)/shard_map/gud,gohdtc->guothc/dot_general | solution.py:47
  127.3 2.0 %broadcast_in_dim.22 = bf16[1,12,2,128,512]{4,3,2,1,0:T(8,128)(2,1)} broadcast(bf16[]{:T(256)} %constant.111.clone.1), dimensions={} | broadcast | bytes 3145730 | tf_op jit(solution)/shard_map/broadcast_in_dim | solution.py:58
  130.2 1.4 copy.65
  132.6 4.4 %collective-permute-start.16 = (bf16[1,3,2,128,512]{3,4,2,1,0:T(8,128)(2,1)S(1)}, bf16[1,3,2,128,512]{3,4,2,1,0:T(8,128)(2,1)S(1)}, u32[]{:S(2)}, u32[]{:S(2)}) collective-permute-start(bf16[1,3,2,128,512]{3,4,2,1,0:T(8,128)(2,1)S(1)} %bitcast.114), channel_id=1, source_target_pairs={{0,24},{8,0},{16,8},{24,16},{1,25},{9,1},{17,9},{25,17},{2,26},{10... | collective-permute-start | bytes 2359304 | tf_op jit(solution)/shard_map/ppermute | solution.py:20
  137.0 2.2 %fusion.58 = bf16[24,7168]{1,0:T(8,128)(2,1)} fusion(bf16[24,7168]{1,0:T(8,128)(2,1)S(1)} %copy-done.1, f32[96,7168]{1,0:T(8,128)} %copy-done, bf16[24,7168]{1,0:T(8,128)(2,1)} %collective-permute-done.13, bf16[24,7168]{1,0:T(8,128)(2,1)} %collective-permute-done.12, f32[7168]{0:T(1024)S(1)} %copy-done.5), kind=kLoop, calls=%fused_computation.45 | loop fusion | flops 1376256 | bytes 2093056 | tf_op jit(solution)/shard_map/convert_element_type | solution.py:197
  139.2 1.4 copy.67
  141.5 5.8 %collective-permute-done.16 = bf16[1,3,2,128,512]{3,4,2,1,0:T(8,128)(2,1)S(1)} collective-permute-done((bf16[1,3,2,128,512]{3,4,2,1,0:T(8,128)(2,1)S(1)}, bf16[1,3,2,128,512]{3,4,2,1,0:T(8,128)(2,1)S(1)}, u32[]{:S(2)}, u32[]{:S(2)}) %collective-permute-start.16) | collective-permute-done | bytes 786464 | tf_op jit(solution)/shard_map/ppermute | solution.py:20
  (96 shorter events, 35.7 us)
Async XLA Ops:
  0.6 11.2 %copy-start.6 = (s32[1,8,1]{1,2,0:T(1,128)S(1)}, s32[1,8,1]{1,2,0:T(1,128)}, u32[]{:S(2)}) copy-start(s32[1,8,1]{1,2,0:T(1,128)} %param.19) | copy-start | bytes 100
  5.0 11.9 %collective-permute-start = (bf16[24,7168]{1,0:T(8,128)(2,1)S(1)}, bf16[24,7168]{1,0:T(8,128)(2,1)S(1)}, u32[]{:S(2)}, u32[]{:S(2)}) collective-permute-start(bf16[24,7168]{1,0:T(8,128)(2,1)S(1)} %get-tuple-element.17), channel_id=1, source_target_pairs={{0,2},{1,3},{2,4},{3,5},{4,6},{5,7},{6,0},{7,1},{8,10},{9,11},{10,... | collective-permute-start | bytes 1032200 | tf_op jit(solution)/shard_map/ppermute | solution.py:81
  7.1 32.3 %collective-permute-start.3 = (bf16[24,7168]{1,0:T(8,128)(2,1)S(1)}, bf16[24,7168]{1,0:T(8,128)(2,1)S(1)}, u32[]{:S(2)}, u32[]{:S(2)}) collective-permute-start(bf16[24,7168]{1,0:T(8,128)(2,1)S(1)} %get-tuple-element.17), channel_id=1, source_target_pairs={{0,1},{1,0},{2,3},{3,2},{4,5},{5,4},{6,7},{7,6},{8,9},{9,8},{10,11... | collective-permute-start | bytes 1032200 | tf_op jit(solution)/shard_map/ppermute | solution.py:75
  16.9 10.1 %collective-permute-start.1 = (bf16[24,7168]{1,0:T(8,128)(2,1)S(1)}, bf16[24,7168]{1,0:T(8,128)(2,1)S(1)}, u32[]{:S(2)}, u32[]{:S(2)}) collective-permute-start(bf16[24,7168]{1,0:T(8,128)(2,1)S(1)} %collective-permute-done), channel_id=1, source_target_pairs={{0,2},{1,3},{2,4},{3,5},{4,6},{5,7},{6,0},{7,1},{8,10},{9,11},{10,... | collective-permute-start | bytes 1032200 | tf_op jit(solution)/shard_map/ppermute | solution.py:81
  17.5 22.8 %collective-permute-start.4 = (bf16[24,7168]{1,0:T(8,128)(2,1)S(1)}, bf16[24,7168]{1,0:T(8,128)(2,1)}, u32[]{:S(2)}, u32[]{:S(2)}) collective-permute-start(bf16[24,7168]{1,0:T(8,128)(2,1)S(1)} %collective-permute-done), channel_id=1, source_target_pairs={{0,1},{1,0},{2,3},{3,2},{4,5},{5,4},{6,7},{7,6},{8,9},{9,8},{10,11... | collective-permute-start | bytes 1032200 | tf_op jit(solution)/shard_map/ppermute | solution.py:75
  27.1 9.3 %collective-permute-start.2 = (bf16[24,7168]{1,0:T(8,128)(2,1)S(1)}, bf16[24,7168]{1,0:T(8,128)(2,1)}, u32[]{:S(2)}, u32[]{:S(2)}) collective-permute-start(bf16[24,7168]{1,0:T(8,128)(2,1)S(1)} %collective-permute-done.1), channel_id=1, source_target_pairs={{0,2},{1,3},{2,4},{3,5},{4,6},{5,7},{6,0},{7,1},{8,10},{9,11},{10,... | collective-permute-start | bytes 1032200 | tf_op jit(solution)/shard_map/ppermute | solution.py:81
  27.1 14.9 %collective-permute-start.5 = (bf16[24,7168]{1,0:T(8,128)(2,1)S(1)}, bf16[24,7168]{1,0:T(8,128)(2,1)}, u32[]{:S(2)}, u32[]{:S(2)}) collective-permute-start(bf16[24,7168]{1,0:T(8,128)(2,1)S(1)} %collective-permute-done.1), channel_id=1, source_target_pairs={{0,1},{1,0},{2,3},{3,2},{4,5},{5,4},{6,7},{7,6},{8,9},{9,8},{10,11... | collective-permute-start | bytes 1032200 | tf_op jit(solution)/shard_map/ppermute | solution.py:75
  31.2 50.5 %all-to-all-start = ((bf16[1,2,4,8,128,128]{5,4,2,1,0,3:T(8,128)(2,1)}), bf16[1,2,4,8,128,128]{5,4,2,1,0,3:T(8,128)(2,1)S(1)}, u32[]{:S(2)}, u32[]{:S(2)}) async-start(bf16[1,2,4,8,128,128]{5,4,2,1,0,3:T(8,128)(2,1)} %copy.53), calls=%async_computation | async-start | bytes 4194304 | tf_op jit(solution)/shard_map/all_to_all | solution.py:145
  36.2 26.5 %copy-start.7 = (f32[1536]{0:T(1024)S(1)}, f32[1536]{0:T(1024)}, u32[]{:S(2)}) copy-start(f32[1536]{0:T(1024)} %param.14) | copy-start | bytes 18436
  36.4 25.6 %collective-permute-start.6 = (bf16[24,7168]{1,0:T(8,128)(2,1)}, bf16[24,7168]{1,0:T(8,128)(2,1)S(1)}, u32[]{:S(2)}, u32[]{:S(2)}) collective-permute-start(bf16[24,7168]{1,0:T(8,128)(2,1)} %collective-permute-done.2), channel_id=1, source_target_pairs={{0,1},{1,0},{2,3},{3,2},{4,5},{5,4},{6,7},{7,6},{8,9},{9,8},{10,11... | collective-permute-start | bytes 1032200 | tf_op jit(solution)/shard_map/ppermute | solution.py:75
  78.3 0.7 copy-start.3
  81.6 1.0 copy-start.4
  83.3 2.6 %slice-start = ((s8[7340032]{0:T(1024)(128)(4,1)}), s8[3145728]{0:T(1024)(128)(4,1)S(1)}, s32[]{:S(2)}) async-start(s8[7340032]{0:T(1024)(128)(4,1)} %bitcast.108), calls=%async_computation.1 | async-start | bytes 6291456
  84.0 2.6 %slice-start.1 = ((s8[7340032]{0:T(1024)(128)(4,1)}), s8[4194304]{0:T(1024)(128)(4,1)S(1)}, s32[]{:S(2)}) async-start(s8[7340032]{0:T(1024)(128)(4,1)} %bitcast.108), calls=%async_computation.2 | async-start | bytes 8388608
  89.0 9.5 %collective-permute-start.7 = (bf16[24,7168]{1,0:T(8,128)(2,1)S(1)}, bf16[24,7168]{1,0:T(8,128)(2,1)S(1)}, u32[]{:S(2)}, u32[]{:S(2)}) collective-permute-start(bf16[24,7168]{1,0:T(8,128)(2,1)S(1)} %get-tuple-element.20), channel_id=1, source_target_pairs={{0,1},{1,0},{2,3},{3,2},{4,5},{5,4},{6,7},{7,6},{8,9},{9,8},{10,11... | collective-permute-start | bytes 1032200 | tf_op jit(solution)/shard_map/ppermute | solution.py:75
  93.8 6.7 %copy-start = (f32[96,7168]{1,0:T(8,128)}, f32[96,7168]{1,0:T(8,128)S(1)}, u32[]{:S(2)}) copy-start(f32[96,7168]{1,0:T(8,128)S(1)} %fusion.70) | copy-start | bytes 8257540
  98.5 9.0 %collective-permute-start.9 = (bf16[24,7168]{1,0:T(8,128)(2,1)}, bf16[24,7168]{1,0:T(8,128)(2,1)S(1)}, u32[]{:S(2)}, u32[]{:S(2)}) collective-permute-start(bf16[24,7168]{1,0:T(8,128)(2,1)} %get-tuple-element.11), channel_id=1, source_target_pairs={{0,1},{1,0},{2,3},{3,2},{4,5},{5,4},{6,7},{7,6},{8,9},{9,8},{10,11... | collective-permute-start | bytes 1032200 | tf_op jit(solution)/shard_map/ppermute | solution.py:75
  101.3 9.0 %collective-permute-start.8 = (bf16[24,7168]{1,0:T(8,128)(2,1)}, bf16[24,7168]{1,0:T(8,128)(2,1)}, u32[]{:S(2)}, u32[]{:S(2)}) collective-permute-start(bf16[24,7168]{1,0:T(8,128)(2,1)} %fusion.64), channel_id=1, source_target_pairs={{0,2},{1,3},{2,4},{3,5},{4,6},{5,7},{6,0},{7,1},{8,10},{9,11},{10,... | collective-permute-start | bytes 1032200 | tf_op jit(solution)/shard_map/ppermute | solution.py:81
  104.1 12.6 %collective-permute-start.14 = (bf16[1,3,2,128,512]{3,4,2,1,0:T(8,128)(2,1)}, bf16[1,3,2,128,512]{3,4,2,1,0:T(8,128)(2,1)}, u32[]{:S(2)}, u32[]{:S(2)}) collective-permute-start(bf16[1,3,2,128,512]{3,4,2,1,0:T(8,128)(2,1)} %bitcast.115), channel_id=1, source_target_pairs={{0,8},{8,16},{16,24},{24,0},{1,9},{9,17},{17,25},{25,1},{2,10},{10... | collective-permute-start | bytes 2359304 | tf_op jit(solution)/shard_map/ppermute | solution.py:20
  107.5 10.0 %collective-permute-start.11 = (bf16[24,7168]{1,0:T(8,128)(2,1)}, bf16[24,7168]{1,0:T(8,128)(2,1)}, u32[]{:S(2)}, u32[]{:S(2)}) collective-permute-start(bf16[24,7168]{1,0:T(8,128)(2,1)} %get-tuple-element.12), channel_id=1, source_target_pairs={{0,1},{1,0},{2,3},{3,2},{4,5},{5,4},{6,7},{7,6},{8,9},{9,8},{10,11... | collective-permute-start | bytes 1032200 | tf_op jit(solution)/shard_map/ppermute | solution.py:75
  112.4 8.2 %collective-permute-start.10 = (bf16[24,7168]{1,0:T(8,128)(2,1)}, bf16[24,7168]{1,0:T(8,128)(2,1)}, u32[]{:S(2)}, u32[]{:S(2)}) collective-permute-start(bf16[24,7168]{1,0:T(8,128)(2,1)} %fusion.63), channel_id=1, source_target_pairs={{0,2},{1,3},{2,4},{3,5},{4,6},{5,7},{6,0},{7,1},{8,10},{9,11},{10,... | collective-permute-start | bytes 1032200 | tf_op jit(solution)/shard_map/ppermute | solution.py:81
  116.7 15.9 %collective-permute-start.15 = (bf16[1,3,2,128,512]{3,4,2,1,0:T(8,128)(2,1)}, bf16[1,3,2,128,512]{3,4,2,1,0:T(8,128)(2,1)}, u32[]{:S(2)}, u32[]{:S(2)}) collective-permute-start(bf16[1,3,2,128,512]{3,4,2,1,0:T(8,128)(2,1)} %bitcast.26), channel_id=1, source_target_pairs={{0,16},{8,24},{16,0},{24,8},{1,17},{9,25},{17,1},{25,9},{2,18},{10... | collective-permute-start | bytes 2359304 | tf_op jit(solution)/shard_map/ppermute | solution.py:20
  117.5 19.5 %collective-permute-start.13 = (bf16[24,7168]{1,0:T(8,128)(2,1)}, bf16[24,7168]{1,0:T(8,128)(2,1)}, u32[]{:S(2)}, u32[]{:S(2)}) collective-permute-start(bf16[24,7168]{1,0:T(8,128)(2,1)} %get-tuple-element.13), channel_id=1, source_target_pairs={{0,1},{1,0},{2,3},{3,2},{4,5},{5,4},{6,7},{7,6},{8,9},{9,8},{10,11... | collective-permute-start | bytes 1032200 | tf_op jit(solution)/shard_map/ppermute | solution.py:75
  122.0 15.0 %collective-permute-start.12 = (bf16[24,7168]{1,0:T(8,128)(2,1)S(1)}, bf16[24,7168]{1,0:T(8,128)(2,1)}, u32[]{:S(2)}, u32[]{:S(2)}) collective-permute-start(bf16[24,7168]{1,0:T(8,128)(2,1)S(1)} %fusion.61), channel_id=1, source_target_pairs={{0,2},{1,3},{2,4},{3,5},{4,6},{5,7},{6,0},{7,1},{8,10},{9,11},{10,... | collective-permute-start | bytes 1032200 | tf_op jit(solution)/shard_map/ppermute | solution.py:81
  125.4 1.2 copy-start.2
  129.3 7.7 %copy-start.1 = (bf16[24,7168]{1,0:T(8,128)(2,1)S(1)}, bf16[24,7168]{1,0:T(8,128)(2,1)}, u32[]{:S(2)}) copy-start(bf16[24,7168]{1,0:T(8,128)(2,1)} %param.10) | copy-start | bytes 1032196
  129.3 7.7 %copy-start.5 = (f32[7168]{0:T(1024)S(1)}, f32[7168]{0:T(1024)}, u32[]{:S(2)}) copy-start(f32[7168]{0:T(1024)} %param.16) | copy-start | bytes 86020
  132.6 14.7 %collective-permute-start.16 = (bf16[1,3,2,128,512]{3,4,2,1,0:T(8,128)(2,1)S(1)}, bf16[1,3,2,128,512]{3,4,2,1,0:T(8,128)(2,1)S(1)}, u32[]{:S(2)}, u32[]{:S(2)}) collective-permute-start(bf16[1,3,2,128,512]{3,4,2,1,0:T(8,128)(2,1)S(1)} %bitcast.114), channel_id=1, source_target_pairs={{0,24},{8,0},{16,8},{24,16},{1,25},{9,1},{17,9},{25,17},{2,26},{10... | collective-permute-start | bytes 2359304 | tf_op jit(solution)/shard_map/ppermute | solution.py:20
where the time goes:
time: 149 us
  waiting for transfers between devices  46 us (31%)
  local copies, waits for them, and re-layouts  36.6 us (25%)
  starting transfers between devices  26.7 us (18%)
  matrix products  24.8 us (17%)
  other arithmetic  13.5 us (9%)
    ppermute x8, waiting for transfers between devices, partner(): return lax.ppermute(x, 'tensor', [(j, j ^ 1) for j in range(tensor_count)])  23 us
    ppermute x6, waiting for transfers between devices, ring(): lax.ppermute(x, 'tensor', [(j, (j // 2 + 1) % rows * 2 + j % 2) for j in...  15 us
    dot_general x1, matrix products, local(): jnp.dot(gathered, qkv_weight, preferred_element_type=jnp.float32) + qkv_bias  13.3 us
    unnamed x28, local copies, waits for them, and re-layouts  13.1 us
    ppermute x8, starting transfers between devices, partner(): return lax.ppermute(x, 'tensor', [(j, j ^ 1) for j in range(tensor_count)])  9.62 us
    ppermute x3, starting transfers between devices, shifted(): return lax.ppermute(x, axis, [(j, (j + k) % n) for j in range(n)])  8.44 us
    dot_general x4, matrix products, send_decode(): jnp.einsum('gud,gohdtc->guothc', placement_index, per_head_rows, preferre...  6.77 us
    ppermute x3, waiting for transfers between devices, shifted(): return lax.ppermute(x, axis, [(j, (j + k) % n) for j in range(n)])  5.83 us
  transfers between devices with their start and end apart: 18, of which 10 were waited for; matrix products, arithmetic and copies ran while one was open for 41% of the time, Pallas kernels for 0%

commit v1 on v0

--- a/solution.py
+++ b/solution.py
@@ -142,7 +142,9 @@
     gathered, source, split = gather_tokens(normed, split)
     if CACHE_STEP == 0:
         gathered, split = lax.optimization_barrier((gathered, split))
-    per_head_rows = lax.all_to_all(split, "tensor", split_axis=3, concat_axis=3, tiled=True)
+    per_head_rows = jnp.concatenate(
+        lax.all_to_all(jnp.stack(jnp.split(split, lax.psum(1, "tensor"), 3), 0), "tensor", 0, 0), 3
+    )
     outgoing = send_decode(per_head_rows, block_dest)
     qkv = (jnp.dot(gathered, qkv_weight, preferred_element_type=jnp.float32) + qkv_bias).astype(
         jnp.bfloat16

time: 149 us -> 161 us (1.081)
  local copies, waits for them, and re-layouts: 36.6 us -> 48.4 us
    unnamed x28 -> x35, local copies, waits for them, and re-layouts: 13.1 us -> 20.9 us
    split x0 -> x9, local copies, waits for them, and re-layouts: none -> 5.24 us  [local(): jnp.split(split, lax.psum(1, 'tensor'), 3)]
    optimization_barrier x1 -> x0, local copies, waits for them, and re-layouts: 2.62 us -> none  [gather_tokens(): own[-1], rider = lax.optimization_barrier((own[-1], rider))]
    all_to_all x1, waiting for transfers between devices: 2.2 us -> 3.95 us  [local(): lax.all_to_all(jnp.stack(jnp.split(split, lax.psum(1, 'tensor'), 3), 0),...]
  transfers between devices with their start and end apart: 18 -> 18, of which waited for: 10 -> 10; matrix products, arithmetic and copies ran while one was open for 41% -> 44% of each run, Pallas kernels for 0% -> 0%
where the time goes in v1:
time: 161 us; the launch traced here: 160 us
  local copies, waits for them, and re-layouts  48.4 us (30%)
  waiting for transfers between devices  46.6 us (29%)
  starting transfers between devices  25.9 us (16%)
  matrix products  24 us (15%)
  other arithmetic  14.2 us (9%)
    ppermute x8, waiting for transfers between devices, partner(): return lax.ppermute(x, 'tensor', [(j, j ^ 1) for j in range(tensor_count)])  22 us
    unnamed x35, local copies, waits for them, and re-layouts  20.9 us
    ppermute x6, waiting for transfers between devices, ring(): lax.ppermute(x, 'tensor', [(j, (j // 2 + 1) % rows * 2 + j % 2) for j in...  14.4 us
    dot_general x1, matrix products, local(): jnp.dot(gathered, qkv_weight, preferred_element_type=jnp.float32) + qkv_bias  12.5 us
    ppermute x8, starting transfers between devices, partner(): return lax.ppermute(x, 'tensor', [(j, j ^ 1) for j in range(tensor_count)])  10.2 us
    ppermute x3, starting transfers between devices, shifted(): return lax.ppermute(x, axis, [(j, (j + k) % n) for j in range(n)])  8.01 us
    dot_general x4, matrix products, send_decode(): jnp.einsum('gud,gohdtc->guothc', placement_index, per_head_rows, preferre...  6.76 us
    ppermute x3, waiting for transfers between devices, shifted(): return lax.ppermute(x, axis, [(j, (j + k) % n) for j in range(n)])  6.26 us
  transfers between devices with their start and end apart: 18, of which 10 were waited for; matrix products, arithmetic and copies ran while one was open for 44% of the time, Pallas kernels for 0%

profile of v1, /device:TPU:1, one launch (start us, length us, event | category | flops | bytes accessed | tf_op | source)
XLA Modules:
  0.0 160.1 jit_solution(18251045343209871782)
XLA Ops:
  3.1 2.1 %constant_dynamic-update-slice_fusion.7 = (bf16[192,7168]{1,0:T(8,128)(2,1)}, bf16[24,7168]{1,0:T(8,128)(2,1)}) fusion(f32[7168]{0:T(1024)} %param.12, f32[7168]{0:T(1024)} %param.11, f32[24]{0:T(128)S(1)} %add_rsqrt_fusion, f32[24]{0:T(128)S(1)} %broadcast_multiply_fusion, bf16[24,7168]{1,0:T(8,128)(2,1)} %param.10), kind=kLoop, calls=%fused_computation.86 | loop fusion | flops 1032191 | bytes 1089728
  5.1 2.1 %collective-permute-start = (bf16[24,7168]{1,0:T(8,128)(2,1)}, bf16[24,7168]{1,0:T(8,128)(2,1)}, u32[]{:S(2)}, u32[]{:S(2)}) collective-permute-start(bf16[24,7168]{1,0:T(8,128)(2,1)} %get-tuple-element.17), channel_id=1, source_target_pairs={{0,2},{1,3},{2,4},{3,5},{4,6},{5,7},{6,0},{7,1},{8,10},{9,11},{10,... | collective-permute-start | bytes 1032200 | tf_op jit(solution)/shard_map/ppermute | solution.py:81
  9.9 2.0 %gather_fusion = s32[192]{0:T(256)S(1)} fusion(s32[192]{0:T(256)} %param.17, s32[1024]{0:T(1024)S(1)} %pad_clamp_fusion), kind=kCustom, calls=%fused_computation | custom fusion | bytes 2304 | tf_op jit(solution)/shard_map/gather | solution.py:155
  12.8 3.1 %copy.249 = bf16[1,1,2,128,4096]{3,4,2,1,0:T(8,128)(2,1)S(1)} copy(bf16[1,1,2,128,4096]{4,3,2,1,0:T(8,128)(2,1)} %param.18) | data formatting | bytes 4194304 | tf_op args[8]
  18.4 1.8 %constant_dynamic-update-slice_fusion.6 = bf16[192,7168]{1,0:T(8,128)(2,1)} fusion(bf16[192,7168]{1,0:T(8,128)(2,1)} %get-tuple-element.16, bf16[24,7168]{1,0:T(8,128)(2,1)} %collective-permute-done), kind=kLoop, calls=%fused_computation.85 | loop fusion | bytes 688128
  20.1 7.7 %collective-permute-done.1 = bf16[24,7168]{1,0:T(8,128)(2,1)} collective-permute-done((bf16[24,7168]{1,0:T(8,128)(2,1)}, bf16[24,7168]{1,0:T(8,128)(2,1)}, u32[]{:S(2)}, u32[]{:S(2)}) %collective-permute-start.1) | collective-permute-done | bytes 344096 | tf_op jit(solution)/shard_map/ppermute | solution.py:81
  28.6 1.8 %constant_dynamic-update-slice_fusion.5 = bf16[192,7168]{1,0:T(8,128)(2,1)} fusion(bf16[192,7168]{1,0:T(8,128)(2,1)} %constant_dynamic-update-slice_fusion.6, bf16[24,7168]{1,0:T(8,128)(2,1)} %collective-permute-done.1), kind=kLoop, calls=%fused_computation.84 | loop fusion | bytes 688128
  41.4 5.0 %all-to-all-start = ((bf16[8,1,2,4,1,128,128]{6,5,3,2,4,1,0:T(8,128)(2,1)}), bf16[8,1,2,4,1,128,128]{6,5,3,2,4,1,0:T(8,128)(2,1)S(1)}, u32[]{:S(2)}, u32[]{:S(2)}) async-start(bf16[8,1,2,4,1,128,128]{6,5,3,2,4,1,0:T(8,128)(2,1)} %bitcast_dynamic-update-slice_fusion), calls=%async_computation | async-start | bytes 4194304 | tf_op jit(solution)/shard_map/all_to_all | solution.py:146
  46.4 1.5 collective-permute-start.6
  47.9 1.8 %constant_dynamic-update-slice_fusion.4 = bf16[192,7168]{1,0:T(8,128)(2,1)} fusion(bf16[192,7168]{1,0:T(8,128)(2,1)} %constant_dynamic-update-slice_fusion.5, bf16[24,7168]{1,0:T(8,128)(2,1)} %collective-permute-done.2), kind=kLoop, calls=%fused_computation.83 | loop fusion | bytes 688128
  49.7 1.7 %constant_dynamic-update-slice_fusion.3 = bf16[192,7168]{1,0:T(8,128)(2,1)} fusion(bf16[192,7168]{1,0:T(8,128)(2,1)} %constant_dynamic-update-slice_fusion.4, bf16[24,7168]{1,0:T(8,128)(2,1)} %collective-permute-done.3), kind=kLoop, calls=%fused_computation.82 | loop fusion | bytes 688128
  51.4 1.7 %constant_dynamic-update-slice_fusion.2 = bf16[192,7168]{1,0:T(8,128)(2,1)} fusion(bf16[192,7168]{1,0:T(8,128)(2,1)} %constant_dynamic-update-slice_fusion.3, bf16[24,7168]{1,0:T(8,128)(2,1)} %collective-permute-done.4), kind=kLoop, calls=%fused_computation.81 | loop fusion | bytes 688128
  53.1 1.7 %constant_dynamic-update-slice_fusion.1 = bf16[192,7168]{1,0:T(8,128)(2,1)} fusion(bf16[192,7168]{1,0:T(8,128)(2,1)} %constant_dynamic-update-slice_fusion.2, bf16[24,7168]{1,0:T(8,128)(2,1)} %collective-permute-done.5), kind=kLoop, calls=%fused_computation.80 | loop fusion | bytes 688128
  54.9 17.3 %collective-permute-done.6 = bf16[24,7168]{1,0:T(8,128)(2,1)S(1)} collective-permute-done((bf16[24,7168]{1,0:T(8,128)(2,1)}, bf16[24,7168]{1,0:T(8,128)(2,1)S(1)}, u32[]{:S(2)}, u32[]{:S(2)}) %collective-permute-start.6) | collective-permute-done | bytes 344096 | tf_op jit(solution)/shard_map/ppermute | solution.py:75
  72.9 12.5 %fusion.2 = bf16[192,1536]{1,0:T(8,128)(2,1)S(1)} fusion(bf16[192,7168]{1,0:T(8,128)(2,1)} %constant_dynamic-update-slice_fusion, bf16[7168,1536]{1,0:T(8,128)(2,1)} %param.13, f32[1536]{0:T(1024)S(1)} %copy-done.7), kind=kOutput, calls=%fused_computation.7 | convolution fusion | flops 4228448256 | bytes 25368576 | tf_op jit(solution)/shard_map/dot_general | solution.py:149
  87.9 3.9 %all-to-all-done = bf16[8,1,2,4,1,128,128]{6,5,3,2,4,1,0:T(8,128)(2,1)S(1)} async-done(((bf16[8,1,2,4,1,128,128]{6,5,3,2,4,1,0:T(8,128)(2,1)}), bf16[8,1,2,4,1,128,128]{6,5,3,2,4,1,0:T(8,128)(2,1)S(1)}, u32[]{:S(2)}, u32[]{:S(2)}) %all-to-all-start) | async-done | bytes 2097184 | tf_op jit(solution)/shard_map/all_to_all | solution.py:146
  100.6 3.4 %collective-permute-start.7 = (bf16[24,7168]{1,0:T(8,128)(2,1)S(1)}, bf16[24,7168]{1,0:T(8,128)(2,1)S(1)}, u32[]{:S(2)}, u32[]{:S(2)}) collective-permute-start(bf16[24,7168]{1,0:T(8,128)(2,1)S(1)} %get-tuple-element.28), channel_id=1, source_target_pairs={{0,1},{1,0},{2,3},{3,2},{4,5},{5,4},{6,7},{7,6},{8,9},{9,8},{10,11... | collective-permute-start | bytes 1032200 | tf_op jit(solution)/shard_map/ppermute | solution.py:75
  105.4 4.7 %collective-permute-done.7 = bf16[24,7168]{1,0:T(8,128)(2,1)S(1)} collective-permute-done((bf16[24,7168]{1,0:T(8,128)(2,1)S(1)}, bf16[24,7168]{1,0:T(8,128)(2,1)S(1)}, u32[]{:S(2)}, u32[]{:S(2)}) %collective-permute-start.7) | collective-permute-done | bytes 344096 | tf_op jit(solution)/shard_map/ppermute | solution.py:75
  110.1 2.0 %collective-permute-start.9 = (bf16[24,7168]{1,0:T(8,128)(2,1)}, bf16[24,7168]{1,0:T(8,128)(2,1)S(1)}, u32[]{:S(2)}, u32[]{:S(2)}) collective-permute-start(bf16[24,7168]{1,0:T(8,128)(2,1)} %get-tuple-element.11), channel_id=1, source_target_pairs={{0,1},{1,0},{2,3},{3,2},{4,5},{5,4},{6,7},{7,6},{8,9},{9,8},{10,11... | collective-permute-start | bytes 1032200 | tf_op jit(solution)/shard_map/ppermute | solution.py:75
  113.4 1.4 fusion.31
  116.2 2.8 %collective-permute-start.14 = (bf16[1,3,2,128,512]{3,4,2,1,0:T(8,128)(2,1)}, bf16[1,3,2,128,512]{3,4,2,1,0:T(8,128)(2,1)}, u32[]{:S(2)}, u32[]{:S(2)}) collective-permute-start(bf16[1,3,2,128,512]{3,4,2,1,0:T(8,128)(2,1)} %bitcast.136), channel_id=1, source_target_pairs={{0,8},{8,16},{16,24},{24,0},{1,9},{9,17},{17,25},{25,1},{2,10},{10... | collective-permute-start | bytes 2359304 | tf_op jit(solution)/shard_map/ppermute | solution.py:20
  119.5 2.4 %collective-permute-done.8 = bf16[24,7168]{1,0:T(8,128)(2,1)} collective-permute-done((bf16[24,7168]{1,0:T(8,128)(2,1)}, bf16[24,7168]{1,0:T(8,128)(2,1)}, u32[]{:S(2)}, u32[]{:S(2)}) %collective-permute-start.8) | collective-permute-done | bytes 344096 | tf_op jit(solution)/shard_map/ppermute | solution.py:81
  121.9 2.0 %fusion.63 = bf16[24,7168]{1,0:T(8,128)(2,1)} fusion(f32[96,7168]{1,0:T(8,128)} %copy-done, bf16[24,7168]{1,0:T(8,128)(2,1)S(1)} %collective-permute-done.9, bf16[24,7168]{1,0:T(8,128)(2,1)} %collective-permute-done.8), kind=kLoop, calls=%fused_computation.54 | loop fusion | flops 860160 | bytes 1720320 | tf_op jit(solution)/shard_map/convert_element_type | solution.py:121
  123.9 1.4 fusion.28
  126.7 1.4 fusion.34
  129.0 3.0 %collective-permute-done.10 = bf16[24,7168]{1,0:T(8,128)(2,1)S(1)} collective-permute-done((bf16[24,7168]{1,0:T(8,128)(2,1)}, bf16[24,7168]{1,0:T(8,128)(2,1)S(1)}, u32[]{:S(2)}, u32[]{:S(2)}) %collective-permute-start.10) | collective-permute-done | bytes 344096 | tf_op jit(solution)/shard_map/ppermute | solution.py:81
  132.0 2.0 %fusion.61 = bf16[24,7168]{1,0:T(8,128)(2,1)} fusion(f32[96,7168]{1,0:T(8,128)} %copy-done, bf16[24,7168]{1,0:T(8,128)(2,1)} %collective-permute-done.11, bf16[24,7168]{1,0:T(8,128)(2,1)S(1)} %collective-permute-done.10), kind=kLoop, calls=%fused_computation.51 | loop fusion | flops 860160 | bytes 1720320 | tf_op jit(solution)/shard_map/convert_element_type | solution.py:121
  134.0 2.4 %fusion.25 = bf16[1,3,2,128,4,128]{5,1,3,4,2,0:T(4,128)(2,1)} fusion(bf16[8,1,2,4,1,128,128]{6,5,3,2,4,1,0:T(8,128)(2,1)S(1)} %all-to-all-done, s32[8]{0:T(128)S(1)} %multiply_add_fusion, s32[3]{0:T(128)S(1)} %iota_add_fusion.1), kind=kOutput, calls=%fused_computation.22 | convolution fusion | flops 6684696 | bytes 2883628 | tf_op jit(solution)/shard_map/gud,gohdtc->guothc/dot_general | solution.py:47
  138.4 2.0 %broadcast_in_dim.22 = bf16[1,12,2,128,512]{4,3,2,1,0:T(8,128)(2,1)} broadcast(bf16[]{:T(256)} %constant.111.clone.1), dimensions={} | broadcast | bytes 3145730 | tf_op jit(solution)/shard_map/broadcast_in_dim | solution.py:58
  144.1 4.4 %collective-permute-start.16 = (bf16[1,3,2,128,512]{3,4,2,1,0:T(8,128)(2,1)S(1)}, bf16[1,3,2,128,512]{3,4,2,1,0:T(8,128)(2,1)S(1)}, u32[]{:S(2)}, u32[]{:S(2)}) collective-permute-start(bf16[1,3,2,128,512]{3,4,2,1,0:T(8,128)(2,1)S(1)} %bitcast.135), channel_id=1, source_target_pairs={{0,24},{8,0},{16,8},{24,16},{1,25},{9,1},{17,9},{25,17},{2,26},{10... | collective-permute-start | bytes 2359304 | tf_op jit(solution)/shard_map/ppermute | solution.py:20
  148.6 2.2 %fusion.58 = bf16[24,7168]{1,0:T(8,128)(2,1)} fusion(bf16[24,7168]{1,0:T(8,128)(2,1)S(1)} %copy-done.1, f32[96,7168]{1,0:T(8,128)} %copy-done, bf16[24,7168]{1,0:T(8,128)(2,1)} %collective-permute-done.13, bf16[24,7168]{1,0:T(8,128)(2,1)} %collective-permute-done.12, f32[7168]{0:T(1024)S(1)} %copy-done.5), kind=kLoop, calls=%fused_computation.46 | loop fusion | flops 1376256 | bytes 2093056 | tf_op jit(solution)/shard_map/convert_element_type | solution.py:199
  153.1 5.7 %collective-permute-done.16 = bf16[1,3,2,128,512]{3,4,2,1,0:T(8,128)(2,1)S(1)} collective-permute-done((bf16[1,3,2,128,512]{3,4,2,1,0:T(8,128)(2,1)S(1)}, bf16[1,3,2,128,512]{3,4,2,1,0:T(8,128)(2,1)S(1)}, u32[]{:S(2)}, u32[]{:S(2)}) %collective-permute-start.16) | collective-permute-done | bytes 786464 | tf_op jit(solution)/shard_map/ppermute | solution.py:20
  (113 shorter events, 47.8 us)
Async XLA Ops:
  0.6 11.3 %copy-start.6 = (s32[1,8,1]{1,2,0:T(1,128)S(1)}, s32[1,8,1]{1,2,0:T(1,128)}, u32[]{:S(2)}) copy-start(s32[1,8,1]{1,2,0:T(1,128)} %param.19) | copy-start | bytes 100
  5.1 12.3 %collective-permute-start = (bf16[24,7168]{1,0:T(8,128)(2,1)}, bf16[24,7168]{1,0:T(8,128)(2,1)}, u32[]{:S(2)}, u32[]{:S(2)}) collective-permute-start(bf16[24,7168]{1,0:T(8,128)(2,1)} %get-tuple-element.17), channel_id=1, source_target_pairs={{0,2},{1,3},{2,4},{3,5},{4,6},{5,7},{6,0},{7,1},{8,10},{9,11},{10,... | collective-permute-start | bytes 1032200 | tf_op jit(solution)/shard_map/ppermute | solution.py:81
  7.2 42.4 %collective-permute-start.3 = (bf16[24,7168]{1,0:T(8,128)(2,1)}, bf16[24,7168]{1,0:T(8,128)(2,1)}, u32[]{:S(2)}, u32[]{:S(2)}) collective-permute-start(bf16[24,7168]{1,0:T(8,128)(2,1)} %get-tuple-element.17), channel_id=1, source_target_pairs={{0,1},{1,0},{2,3},{3,2},{4,5},{5,4},{6,7},{7,6},{8,9},{9,8},{10,11... | collective-permute-start | bytes 1032200 | tf_op jit(solution)/shard_map/ppermute | solution.py:75
  17.4 10.4 %collective-permute-start.1 = (bf16[24,7168]{1,0:T(8,128)(2,1)}, bf16[24,7168]{1,0:T(8,128)(2,1)}, u32[]{:S(2)}, u32[]{:S(2)}) collective-permute-start(bf16[24,7168]{1,0:T(8,128)(2,1)} %collective-permute-done), channel_id=1, source_target_pairs={{0,2},{1,3},{2,4},{3,5},{4,6},{5,7},{6,0},{7,1},{8,10},{9,11},{10,... | collective-permute-start | bytes 1032200 | tf_op jit(solution)/shard_map/ppermute | solution.py:81
  17.5 33.9 %collective-permute-start.4 = (bf16[24,7168]{1,0:T(8,128)(2,1)}, bf16[24,7168]{1,0:T(8,128)(2,1)}, u32[]{:S(2)}, u32[]{:S(2)}) collective-permute-start(bf16[24,7168]{1,0:T(8,128)(2,1)} %collective-permute-done), channel_id=1, source_target_pairs={{0,1},{1,0},{2,3},{3,2},{4,5},{5,4},{6,7},{7,6},{8,9},{9,8},{10,11... | collective-permute-start | bytes 1032200 | tf_op jit(solution)/shard_map/ppermute | solution.py:75
  27.8 18.6 %collective-permute-start.2 = (bf16[24,7168]{1,0:T(8,128)(2,1)}, bf16[24,7168]{1,0:T(8,128)(2,1)}, u32[]{:S(2)}, u32[]{:S(2)}) collective-permute-start(bf16[24,7168]{1,0:T(8,128)(2,1)} %collective-permute-done.1), channel_id=1, source_target_pairs={{0,2},{1,3},{2,4},{3,5},{4,6},{5,7},{6,0},{7,1},{8,10},{9,11},{10,... | collective-permute-start | bytes 1032200 | tf_op jit(solution)/shard_map/ppermute | solution.py:81
  27.8 25.3 %collective-permute-start.5 = (bf16[24,7168]{1,0:T(8,128)(2,1)}, bf16[24,7168]{1,0:T(8,128)(2,1)}, u32[]{:S(2)}, u32[]{:S(2)}) collective-permute-start(bf16[24,7168]{1,0:T(8,128)(2,1)} %collective-permute-done.1), channel_id=1, source_target_pairs={{0,1},{1,0},{2,3},{3,2},{4,5},{5,4},{6,7},{7,6},{8,9},{9,8},{10,11... | collective-permute-start | bytes 1032200 | tf_op jit(solution)/shard_map/ppermute | solution.py:75
  41.4 50.5 %all-to-all-start = ((bf16[8,1,2,4,1,128,128]{6,5,3,2,4,1,0:T(8,128)(2,1)}), bf16[8,1,2,4,1,128,128]{6,5,3,2,4,1,0:T(8,128)(2,1)S(1)}, u32[]{:S(2)}, u32[]{:S(2)}) async-start(bf16[8,1,2,4,1,128,128]{6,5,3,2,4,1,0:T(8,128)(2,1)} %bitcast_dynamic-update-slice_fusion), calls=%async_computation | async-start | bytes 4194304 | tf_op jit(solution)/shard_map/all_to_all | solution.py:146
  46.4 26.5 %copy-start.7 = (f32[1536]{0:T(1024)S(1)}, f32[1536]{0:T(1024)}, u32[]{:S(2)}) copy-start(f32[1536]{0:T(1024)} %param.14) | copy-start | bytes 18436
  46.4 25.8 %collective-permute-start.6 = (bf16[24,7168]{1,0:T(8,128)(2,1)}, bf16[24,7168]{1,0:T(8,128)(2,1)S(1)}, u32[]{:S(2)}, u32[]{:S(2)}) collective-permute-start(bf16[24,7168]{1,0:T(8,128)(2,1)} %collective-permute-done.2), channel_id=1, source_target_pairs={{0,1},{1,0},{2,3},{3,2},{4,5},{5,4},{6,7},{7,6},{8,9},{9,8},{10,11... | collective-permute-start | bytes 1032200 | tf_op jit(solution)/shard_map/ppermute | solution.py:75
  86.7 0.7 copy-start.3
  93.2 1.0 copy-start.4
  94.9 2.7 %slice-start = ((s8[7340032]{0:T(1024)(128)(4,1)}), s8[3145728]{0:T(1024)(128)(4,1)S(1)}, s32[]{:S(2)}) async-start(s8[7340032]{0:T(1024)(128)(4,1)} %bitcast.128), calls=%async_computation.1 | async-start | bytes 6291456
  95.6 2.6 %slice-start.1 = ((s8[7340032]{0:T(1024)(128)(4,1)}), s8[4194304]{0:T(1024)(128)(4,1)S(1)}, s32[]{:S(2)}) async-start(s8[7340032]{0:T(1024)(128)(4,1)} %bitcast.128), calls=%async_computation.2 | async-start | bytes 8388608
  100.6 9.5 %collective-permute-start.7 = (bf16[24,7168]{1,0:T(8,128)(2,1)S(1)}, bf16[24,7168]{1,0:T(8,128)(2,1)S(1)}, u32[]{:S(2)}, u32[]{:S(2)}) collective-permute-start(bf16[24,7168]{1,0:T(8,128)(2,1)S(1)} %get-tuple-element.28), channel_id=1, source_target_pairs={{0,1},{1,0},{2,3},{3,2},{4,5},{5,4},{6,7},{7,6},{8,9},{9,8},{10,11... | collective-permute-start | bytes 1032200 | tf_op jit(solution)/shard_map/ppermute | solution.py:75
  105.4 6.7 %copy-start = (f32[96,7168]{1,0:T(8,128)}, f32[96,7168]{1,0:T(8,128)S(1)}, u32[]{:S(2)}) copy-start(f32[96,7168]{1,0:T(8,128)S(1)} %fusion.70) | copy-start | bytes 8257540
  110.1 9.0 %collective-permute-start.9 = (bf16[24,7168]{1,0:T(8,128)(2,1)}, bf16[24,7168]{1,0:T(8,128)(2,1)S(1)}, u32[]{:S(2)}, u32[]{:S(2)}) collective-permute-start(bf16[24,7168]{1,0:T(8,128)(2,1)} %get-tuple-element.11), channel_id=1, source_target_pairs={{0,1},{1,0},{2,3},{3,2},{4,5},{5,4},{6,7},{7,6},{8,9},{9,8},{10,11... | collective-permute-start | bytes 1032200 | tf_op jit(solution)/shard_map/ppermute | solution.py:75
  112.9 9.0 %collective-permute-start.8 = (bf16[24,7168]{1,0:T(8,128)(2,1)}, bf16[24,7168]{1,0:T(8,128)(2,1)}, u32[]{:S(2)}, u32[]{:S(2)}) collective-permute-start(bf16[24,7168]{1,0:T(8,128)(2,1)} %fusion.64), channel_id=1, source_target_pairs={{0,2},{1,3},{2,4},{3,5},{4,6},{5,7},{6,0},{7,1},{8,10},{9,11},{10,... | collective-permute-start | bytes 1032200 | tf_op jit(solution)/shard_map/ppermute | solution.py:81
  116.2 12.1 %collective-permute-start.14 = (bf16[1,3,2,128,512]{3,4,2,1,0:T(8,128)(2,1)}, bf16[1,3,2,128,512]{3,4,2,1,0:T(8,128)(2,1)}, u32[]{:S(2)}, u32[]{:S(2)}) collective-permute-start(bf16[1,3,2,128,512]{3,4,2,1,0:T(8,128)(2,1)} %bitcast.136), channel_id=1, source_target_pairs={{0,8},{8,16},{16,24},{24,0},{1,9},{9,17},{17,25},{25,1},{2,10},{10... | collective-permute-start | bytes 2359304 | tf_op jit(solution)/shard_map/ppermute | solution.py:20
  119.0 10.0 %collective-permute-start.11 = (bf16[24,7168]{1,0:T(8,128)(2,1)}, bf16[24,7168]{1,0:T(8,128)(2,1)}, u32[]{:S(2)}, u32[]{:S(2)}) collective-permute-start(bf16[24,7168]{1,0:T(8,128)(2,1)} %get-tuple-element.12), channel_id=1, source_target_pairs={{0,1},{1,0},{2,3},{3,2},{4,5},{5,4},{6,7},{7,6},{8,9},{9,8},{10,11... | collective-permute-start | bytes 1032200 | tf_op jit(solution)/shard_map/ppermute | solution.py:75
  123.9 8.1 %collective-permute-start.10 = (bf16[24,7168]{1,0:T(8,128)(2,1)}, bf16[24,7168]{1,0:T(8,128)(2,1)S(1)}, u32[]{:S(2)}, u32[]{:S(2)}) collective-permute-start(bf16[24,7168]{1,0:T(8,128)(2,1)} %fusion.63), channel_id=1, source_target_pairs={{0,2},{1,3},{2,4},{3,5},{4,6},{5,7},{6,0},{7,1},{8,10},{9,11},{10,... | collective-permute-start | bytes 1032200 | tf_op jit(solution)/shard_map/ppermute | solution.py:81
  128.3 15.8 %collective-permute-start.15 = (bf16[1,3,2,128,512]{3,4,2,1,0:T(8,128)(2,1)}, bf16[1,3,2,128,512]{3,4,2,1,0:T(8,128)(2,1)}, u32[]{:S(2)}, u32[]{:S(2)}) collective-permute-start(bf16[1,3,2,128,512]{3,4,2,1,0:T(8,128)(2,1)} %bitcast.36), channel_id=1, source_target_pairs={{0,16},{8,24},{16,0},{24,8},{1,17},{9,25},{17,1},{25,9},{2,18},{10... | collective-permute-start | bytes 2359304 | tf_op jit(solution)/shard_map/ppermute | solution.py:20
  129.0 19.6 %collective-permute-start.13 = (bf16[24,7168]{1,0:T(8,128)(2,1)}, bf16[24,7168]{1,0:T(8,128)(2,1)}, u32[]{:S(2)}, u32[]{:S(2)}) collective-permute-start(bf16[24,7168]{1,0:T(8,128)(2,1)} %get-tuple-element.13), channel_id=1, source_target_pairs={{0,1},{1,0},{2,3},{3,2},{4,5},{5,4},{6,7},{7,6},{8,9},{9,8},{10,11... | collective-permute-start | bytes 1032200 | tf_op jit(solution)/shard_map/ppermute | solution.py:75
  134.0 14.5 %collective-permute-start.12 = (bf16[24,7168]{1,0:T(8,128)(2,1)}, bf16[24,7168]{1,0:T(8,128)(2,1)}, u32[]{:S(2)}, u32[]{:S(2)}) collective-permute-start(bf16[24,7168]{1,0:T(8,128)(2,1)} %fusion.61), channel_id=1, source_target_pairs={{0,2},{1,3},{2,4},{3,5},{4,6},{5,7},{6,0},{7,1},{8,10},{9,11},{10,... | collective-permute-start | bytes 1032200 | tf_op jit(solution)/shard_map/ppermute | solution.py:81
  136.5 1.2 copy-start.2
  140.4 8.2 %copy-start.1 = (bf16[24,7168]{1,0:T(8,128)(2,1)S(1)}, bf16[24,7168]{1,0:T(8,128)(2,1)}, u32[]{:S(2)}) copy-start(bf16[24,7168]{1,0:T(8,128)(2,1)} %param.10) | copy-start | bytes 1032196
  140.4 8.2 %copy-start.5 = (f32[7168]{0:T(1024)S(1)}, f32[7168]{0:T(1024)}, u32[]{:S(2)}) copy-start(f32[7168]{0:T(1024)} %param.16) | copy-start | bytes 86020
  144.1 14.7 %collective-permute-start.16 = (bf16[1,3,2,128,512]{3,4,2,1,0:T(8,128)(2,1)S(1)}, bf16[1,3,2,128,512]{3,4,2,1,0:T(8,128)(2,1)S(1)}, u32[]{:S(2)}, u32[]{:S(2)}) collective-permute-start(bf16[1,3,2,128,512]{3,4,2,1,0:T(8,128)(2,1)S(1)} %bitcast.135), channel_id=1, source_target_pairs={{0,24},{8,0},{16,8},{24,16},{1,25},{9,1},{17,9},{25,17},{2,26},{10... | collective-permute-start | bytes 2359304 | tf_op jit(solution)/shard_map/ppermute | solution.py:20
